TPU v7x, 256 devices: a whole 4x4x8 slice. The times are simulated.
256 devices in a mesh: dp: 16 (over x, y_hi, core), seq: 16 (over z, y_lo).
Axes of the slice: x: 4, y: 4 (y_hi: 2, y_lo: 2; y = y_hi * 2 + y_lo), z: 8, core: 2. Of those that a mesh axis runs over, the one named last changes fastest.
Arguments:
- queries: bfloat16 [40960, 768], P(('dp', 'seq')), may hold values from -8 to 8
- keys: bfloat16 [40960, 768], P(('dp', 'seq')), may hold values from -8 to 8
- values: bfloat16 [40960, 768], P(('dp', 'seq')), may hold values from -6 to 6
- frames: bfloat16 [40960, 768], P(('dp', 'seq')), may hold values from -4 to 4
- upstream: bfloat16 [40960, 768], P(('dp', 'seq')), may hold values from -6 to 6
- lengths: int32 [16], P('dp'), may hold values from 640 to 2560, as said below
- conv_kernel: bfloat16 [32, 768], replicated, may hold values from -1 to 1
Outputs:
- out: bfloat16 [40960, 768], P(('dp', 'seq'))
- query_grad: bfloat16 [40960, 768], P(('dp', 'seq'))
- key_grad: bfloat16 [40960, 768], P(('dp', 'seq'))
- value_grad: bfloat16 [40960, 768], P(('dp', 'seq'))
- frame_grad: bfloat16 [40960, 768], P(('dp', 'seq'))
- kernel_grad: float32 [32, 768], replicated
Inputs may be any that keep to these rules, and one draw needn't show every extreme that they name: `lengths`: one utterance has all 2560 frames live and another has 640.
All inputs are finite; a program needn't handle non-finite values.
Results may differ from a plain program's by a relative error of at most 0.0262.
Values may be sent and summed in bfloat16 or wider, within the bound.
No kernel may reach another device: no remote copies, remote signals or barrier semaphores. Data moves between devices by JAX's collectives and lax.ppermute only.
A program may use at most 128 MiB of HBM per device.

v0:
```python
import jax
import jax.numpy as jnp
from jax import lax
from jax.sharding import Mesh
from jax.sharding import PartitionSpec as P

HEAD_DIM = 64
KERNEL = 32
GROUPS = 4


def shifted(x, axis, by):
    count = lax.axis_size(axis)
    pairs = [(i, i + by) for i in range(count) if 0 <= i + by < count]
    return lax.ppermute(x, axis, pairs)


def butterfly_sum(x, axes):
    for axis in axes:
        count = lax.axis_size(axis)
        step = 1
        while step < count:
            x = x + lax.ppermute(x, axis, [(i, i ^ step) for i in range(count)])
            step = step * 2
    return x


def per_device(queries, keys, values, frames, upstream, lengths, conv_kernel):
    rows = queries.shape[0]
    channels = queries.shape[1]
    sub_count = lax.axis_size("sb")
    block_count_a = lax.axis_size("sa")
    group = channels // sub_count
    head_count = group // HEAD_DIM
    row_count = rows * sub_count
    span = row_count * block_count_a
    block_index = lax.axis_index("sa")
    group_index = lax.axis_index("sb")
    first_row = block_index * row_count
    length = lengths[0]
    score_scale = HEAD_DIM ** (-0.5)
    stacked = jnp.stack([queries, keys, values, frames, upstream])
    mixed = lax.all_to_all(
        stacked.reshape(5, rows, sub_count, group), "sb", 2, 1, tiled=True
    ).reshape(5, row_count, group)
    queries_b = mixed[0]
    frames_b = mixed[3]
    upstream_b = mixed[4]
    kv_all = lax.all_gather(jnp.concatenate([mixed[1], mixed[2]], axis=1), "sa", axis=0, tiled=True)
    key_all = kv_all[:, :group]
    value_all = kv_all[:, group:]
    key_block = row_count
    block_count = span // key_block
    key_blocks = key_all.reshape(block_count, key_block, head_count, HEAD_DIM)
    value_blocks = value_all.reshape(block_count, key_block, head_count, HEAD_DIM)
    block_starts = jnp.arange(block_count, dtype=jnp.int32) * key_block
    query_heads = queries_b.reshape(row_count, head_count, HEAD_DIM)

    def block_scores(key_part, block_start):
        scores = (
            jnp.einsum("thd,khd->htk", query_heads, key_part, preferred_element_type=jnp.float32)
            * score_scale
        )
        key_live = block_start + jnp.arange(key_part.shape[0], dtype=jnp.int32) < length
        return jnp.where(key_live[None, None, :], scores, -jnp.inf)

    def running_total(state_pair, block_items):
        running_top, total_sum = state_pair
        key_part, block_start = block_items
        scores = block_scores(key_part, block_start)
        higher = jnp.maximum(running_top, jnp.max(scores, axis=2))
        total_sum = total_sum * jnp.exp(running_top - higher) + jnp.sum(
            jnp.exp(scores - higher[:, :, None]), axis=2
        )
        return ((higher, total_sum), None)

    start_state = (
        jnp.full((head_count, row_count), -1e30, jnp.float32),
        jnp.zeros((head_count, row_count), jnp.float32),
    )
    (running_top, total_sum), unused = lax.scan(
        running_total, start_state, (key_blocks, block_starts)
    )
    log_total = running_top + jnp.log(total_sum)

    def attend_block(attend_acc, block_items):
        key_part, value_part, block_start = block_items
        prob_bf = jnp.exp(block_scores(key_part, block_start) - log_total[:, :, None]).astype(
            jnp.bfloat16
        )
        return (
            attend_acc
            + jnp.einsum("htk,khd->thd", prob_bf, value_part, preferred_element_type=jnp.float32),
            None,
        )

    attend_acc, unused = lax.scan(
        attend_block,
        jnp.zeros((row_count, head_count, HEAD_DIM), jnp.float32),
        (key_blocks, value_blocks, block_starts),
    )
    attended = attend_acc.reshape(row_count, group).astype(jnp.bfloat16)
    frame_live = (first_row + jnp.arange(row_count, dtype=jnp.int32) < length)[:, None]
    hidden = (frames_b.astype(jnp.float32) + attended.astype(jnp.float32)).astype(jnp.bfloat16)
    masked = jnp.where(frame_live, hidden, jnp.zeros_like(hidden))
    past_rows = shifted(masked[row_count - (KERNEL - 1) :], "sa", 1)
    extended = jnp.concatenate([past_rows, masked], axis=0).astype(jnp.float32)
    weights = lax.dynamic_slice_in_dim(conv_kernel, group_index * group, group, axis=1).astype(
        jnp.float32
    )
    conv_out = jnp.zeros((row_count, group), jnp.float32)
    for tap_index in range(KERNEL):
        conv_out = (
            conv_out
            + weights[tap_index]
            * extended[KERNEL - 1 - tap_index : KERNEL - 1 - tap_index + row_count]
        )
    sig_conv = jax.nn.sigmoid(conv_out)
    out = (hidden.astype(jnp.float32) + conv_out * sig_conv).astype(jnp.bfloat16)
    loss_grad = jnp.where(frame_live, upstream_b.astype(jnp.float32), 0.0)
    conv_grad = (loss_grad * sig_conv * (1.0 + conv_out * (1.0 - sig_conv))).astype(jnp.bfloat16)
    conv_float = conv_grad.astype(jnp.float32)
    kernel_part = jnp.stack(
        [
            jnp.sum(
                conv_float * extended[KERNEL - 1 - tap_index : KERNEL - 1 - tap_index + row_count],
                axis=0,
            )
            for tap_index in range(KERNEL)
        ]
    )
    future_rows = shifted(conv_grad[: KERNEL - 1], "sa", -1)
    ahead_rows = jnp.concatenate([conv_grad, future_rows], axis=0).astype(jnp.float32)
    back_conv = jnp.zeros((row_count, group), jnp.float32)
    for tap_index in range(KERNEL):
        back_conv = back_conv + weights[tap_index] * ahead_rows[tap_index : tap_index + row_count]
    frame_grad = (loss_grad + jnp.where(frame_live, back_conv, 0.0)).astype(jnp.bfloat16)
    grad_heads = frame_grad.reshape(row_count, head_count, HEAD_DIM)
    attended_heads = attended.reshape(row_count, head_count, HEAD_DIM)
    delta_rows = jnp.sum(
        grad_heads.astype(jnp.float32) * attended_heads.astype(jnp.float32), axis=2
    ).T

    def score_grads(key_part, value_part, block_start):
        soft_weights = jnp.exp(block_scores(key_part, block_start) - log_total[:, :, None])
        prob_grad = jnp.einsum(
            "thd,khd->htk", grad_heads, value_part, preferred_element_type=jnp.float32
        )
        score_grad = (soft_weights * (prob_grad - delta_rows[:, :, None])).astype(jnp.bfloat16)
        return (soft_weights.astype(jnp.bfloat16), score_grad)

    def gradient_block(query_acc, block_items):
        key_part, value_part, block_start = block_items
        prob_bf, score_grad = score_grads(key_part, value_part, block_start)
        query_acc = query_acc + jnp.einsum(
            "htk,khd->thd", score_grad, key_part, preferred_element_type=jnp.float32
        )
        key_term = (
            jnp.einsum("htk,thd->khd", score_grad, query_heads, preferred_element_type=jnp.float32)
            * score_scale
        )
        value_term = jnp.einsum(
            "htk,thd->khd", prob_bf, grad_heads, preferred_element_type=jnp.float32
        )
        grad_terms = jnp.concatenate(
            [key_term.reshape(key_block, group), value_term.reshape(key_block, group)], axis=1
        )
        return (query_acc, grad_terms)

    query_acc, grad_terms = lax.scan(
        gradient_block,
        jnp.zeros((row_count, head_count, HEAD_DIM), jnp.float32),
        (key_blocks, value_blocks, block_starts),
    )
    own_rows = lax.psum_scatter(
        grad_terms.reshape(span, 2 * group).astype(jnp.bfloat16),
        "sa",
        scatter_dimension=0,
        tiled=True,
    ).astype(jnp.float32)
    key_grad = own_rows[:, :group].astype(jnp.bfloat16)
    value_grad = own_rows[:, group:].astype(jnp.bfloat16)
    query_grad = (query_acc * score_scale).reshape(row_count, group).astype(jnp.bfloat16)
    kernel_full = lax.dynamic_update_slice_in_dim(
        jnp.zeros((KERNEL, channels), jnp.float32), kernel_part, group_index * group, axis=1
    )
    kernel_total = butterfly_sum(kernel_full, ("sb", "sa", "dp"))
    kernel_grad = kernel_total / lax.axis_size("dp")
    results = jnp.stack([out, query_grad, key_grad, value_grad, frame_grad])
    spread = lax.all_to_all(
        results.reshape(5, sub_count, rows, 1, group), "sb", 1, 3, tiled=True
    ).reshape(5, rows, channels)
    return (spread[0], spread[1], spread[2], spread[3], spread[4], kernel_grad)


def solution(mesh):
    seq_count = mesh.shape["seq"]
    split_mesh = Mesh(
        mesh.devices.reshape(mesh.shape["dp"], seq_count // GROUPS, GROUPS), ("dp", "sa", "sb")
    )
    rows_spec = P(("dp", "sa", "sb"), None)
    placed = (rows_spec, rows_spec, rows_spec, rows_spec, rows_spec, P("dp"), P())
    return jax.shard_map(
        per_device,
        mesh=split_mesh,
        in_specs=placed,
        out_specs=(rows_spec, rows_spec, rows_spec, rows_spec, rows_spec, P()),
        check_vma=False,
    )
```

profile of v0, /device:TPU:2, one launch (start us, length us, event | category | flops | bytes accessed | tf_op | source)
XLA Modules:
  0.0 392.6 jit_solution(232273346341479808)
XLA Ops:
  12.7 24.6 %all_to_all.30 = bf16[5,160,4,192]{3,1,0,2:T(8,128)(2,1)S(1)} all-to-all(bf16[5,160,4,192]{3,1,0,2:T(8,128)(2,1)S(1)} %copy.80), channel_id=1, replica_groups=mesh['dp'=16,'sa'=4,'sb'=4] {'sb'}, dimensions={2} | all-to-all | bytes 2457600 | tf_op jit(solution)/shard_map/all_to_all | solution.py:43
  41.8 47.3 %all-gather.2.cloned.1.call-done = bf16[2560,384]{1,0:T(8,128)(2,1)} async-done(((bf16[640,384]{1,0:T(8,128)(2,1)}), bf16[2560,384]{1,0:T(8,128)(2,1)}) %all-gather.2.cloned.1.call-update) | async-done | bytes 1966096 | tf_op jit(solution)/shard_map/all_gather | solution.py:49
  89.1 2.3 fusion.111
  91.4 1.4 copy.82
  92.8 1.9 reshape.121
  95.8 40.8 %while.37 = (s32[]{:T(128)}, f32[3,640]{1,0:T(4,128)S(1)}, f32[3,640]{1,0:T(4,128)S(1)}, s32[4]{0:T(128)}, s32[]{:T(128)}, /*index=5*/bf16[4,640,3,64]{1,3,2,0:T...) while((s32[]{:T(128)}, f32[3,640]{1,0:T(4,128)S(1)}, f32[3,640]{1,0:T(4,128)S(1)}, ...), condition=%wide.region_3.4_spmd.clone, body=%wide.region_0.3_spmd.clone.sunk | while | flops 165898880 | bytes 10424316 | solution.py:81
  98.4 4.1 %bitcast_reduce_fusion.2 = (f32[3,640]{1,0:T(4,128)S(1)}, f32[3,640,640]{2,1,0:T(8,128)}) fusion(pred[640]{0:T(1024)(128)(4,1)S(1)} %add_compare_fusion.7, bf16[640,3,64]{0,2,1:T(8,128)(2,1)S(1)} %get-tuple-element.670, bf16[4,640,3,64]{1,3,2,0:T(8,128)(2,1)} %get-tuple-element.669, s32[]{:T(128)} %get-tuple-element.655), kind=kOutput, calls=%fused_computation.1.clone.1 | convolution fusion | flops 160970880 | bytes 5415552 | tf_op jit(solution)/shard_map/while/body/eval_jaxpr/thd,khd->htk/dot_general | solution.py:61
  102.5 3.4 fusion.146
  108.6 4.1 %bitcast_reduce_fusion.2 = (f32[3,640]{1,0:T(4,128)S(1)}, f32[3,640,640]{2,1,0:T(8,128)}) fusion(pred[640]{0:T(1024)(128)(4,1)S(1)} %add_compare_fusion.7, bf16[640,3,64]{0,2,1:T(8,128)(2,1)S(1)} %get-tuple-element.670, bf16[4,640,3,64]{1,3,2,0:T(8,128)(2,1)} %get-tuple-element.669, s32[]{:T(128)} %get-tuple-element.655), kind=kOutput, calls=%fused_computation.1.clone.1 | convolution fusion | flops 160970880 | bytes 5415552 | tf_op jit(solution)/shard_map/while/body/eval_jaxpr/thd,khd->htk/dot_general | solution.py:61
  112.7 3.4 fusion.146
  118.8 4.1 %bitcast_reduce_fusion.2 = (f32[3,640]{1,0:T(4,128)S(1)}, f32[3,640,640]{2,1,0:T(8,128)}) fusion(pred[640]{0:T(1024)(128)(4,1)S(1)} %add_compare_fusion.7, bf16[640,3,64]{0,2,1:T(8,128)(2,1)S(1)} %get-tuple-element.670, bf16[4,640,3,64]{1,3,2,0:T(8,128)(2,1)} %get-tuple-element.669, s32[]{:T(128)} %get-tuple-element.655), kind=kOutput, calls=%fused_computation.1.clone.1 | convolution fusion | flops 160970880 | bytes 5415552 | tf_op jit(solution)/shard_map/while/body/eval_jaxpr/thd,khd->htk/dot_general | solution.py:61
  123.0 3.4 fusion.146
  129.0 4.1 %bitcast_reduce_fusion.2 = (f32[3,640]{1,0:T(4,128)S(1)}, f32[3,640,640]{2,1,0:T(8,128)}) fusion(pred[640]{0:T(1024)(128)(4,1)S(1)} %add_compare_fusion.7, bf16[640,3,64]{0,2,1:T(8,128)(2,1)S(1)} %get-tuple-element.670, bf16[4,640,3,64]{1,3,2,0:T(8,128)(2,1)} %get-tuple-element.669, s32[]{:T(128)} %get-tuple-element.655), kind=kOutput, calls=%fused_computation.1.clone.1 | convolution fusion | flops 160970880 | bytes 5415552 | tf_op jit(solution)/shard_map/while/body/eval_jaxpr/thd,khd->htk/dot_general | solution.py:61
  133.2 3.4 fusion.146
  138.2 24.5 %while.38 = (s32[]{:T(128)}, f32[640,3,64]{0,2,1:T(8,128)}, bf16[4,640,3,64]{1,3,2,0:T(8,128)(2,1)S(1)}, s32[4]{0:T(128)}, s32[]{:T(128)}, /*index=5*/bf16[4,640...) while((s32[]{:T(128)}, f32[640,3,64]{0,2,1:T(8,128)}, ...), condition=%wide.region_5.6_spmd.clone, body=%wide.region_4.5_spmd.clone.sunk | while | flops 319735040 | bytes 1733379 | solution.py:97
  140.8 3.4 fusion.151
  146.8 3.6 fusion.151
  152.9 3.6 fusion.151
  159.1 3.6 fusion.151
  165.3 5.2 %collective-permute-start = (bf16[31,192]{1,0:T(8,128)(2,1)S(1)}, bf16[31,192]{1,0:T(8,128)(2,1)S(1)}, u32[]{:S(2)}, u32[]{:S(2)}) collective-permute-start(bf16[31,192]{1,0:T(8,128)(2,1)S(1)} %slice.531), channel_id=1, source_target_pairs={{0,4},{4,8},{8,12},{1,5},{5,9},{9,13},{2,6},{6,10},{10,14},{3,7},{... | collective-permute-start | bytes 35720 | tf_op jit(solution)/shard_map/ppermute | solution.py:15
  172.1 7.1 %fusion.71 = (f32[192]{0:T(256)}, f32[192]{0:T(256)}, f32[192]{0:T(256)}, f32[192]{0:T(256)}, f32[192]{0:T(256)}, /*index=5*/f32[192]{0:T(256)}, f32[192]{0:T(25...) fusion(f32[671,192]{1,0:T(8,128)S(1)} %maximum_convert_fusion, ...), kind=kLoop, calls=%fused_computation.113 | loop fusion | flops 13636224 | bytes 16750720 | tf_op jit(solution)/shard_map/reduce_sum | solution.py:125
  180.5 5.6 %collective-permute-done.1 = bf16[31,192]{1,0:T(8,128)(2,1)S(1)} collective-permute-done((bf16[31,192]{1,0:T(8,128)(2,1)S(1)}, bf16[31,192]{1,0:T(8,128)(2,1)S(1)}, u32[]{:S(2)}, u32[]{:S(2)}) %collective-permute-start.1) | collective-permute-done | bytes 11936 | tf_op jit(solution)/shard_map/ppermute | solution.py:15
  186.2 3.1 fusion.75
  191.2 70.0 %while.39 = (s32[]{:T(128)}, f32[640,3,64]{0,2,1:T(8,128)}, bf16[4,640,384]{2,1,0:T(8,128)(2,1)}, bf16[4,640,3,64]{1,3,2,0:T(8,128)(2,1)}, s32[4]{0:T(128)}, /*i...) while((s32[]{:T(128)}, f32[640,3,64]{0,2,1:T(8,128)}, ...), condition=%wide.region_8.9_spmd.clone, body=%wide.region_7.8_spmd.clone.sunk | while | flops 800195840 | bytes 28292124 | solution.py:170
  191.2 1.8 fusion.162
  195.7 2.7 multiply_convert_fusion.3
  199.3 2.3 fusion.164
  202.4 2.0 copy.135
  204.4 1.8 constant_dynamic-update-slice_fusion.12
  206.3 2.3 fusion.163
  208.6 1.8 fusion.162
  213.0 2.7 multiply_convert_fusion.3
  216.6 2.3 fusion.164
  219.7 2.0 copy.135
  221.8 1.9 constant_dynamic-update-slice_fusion.12
  223.6 2.5 fusion.163
  226.1 1.8 fusion.162
  230.6 2.7 multiply_convert_fusion.3
  234.2 2.3 fusion.164
  237.3 2.0 copy.135
  239.3 1.9 constant_dynamic-update-slice_fusion.12
  241.2 2.5 fusion.163
  243.7 1.8 fusion.162
  248.1 2.7 multiply_convert_fusion.3
  251.7 2.3 fusion.164
  254.8 2.0 copy.135
  256.9 1.9 constant_dynamic-update-slice_fusion.12
  258.7 2.5 fusion.163
  261.2 2.9 fusion.70
  264.8 44.9 %reduce-scatter.2.cloned.1.call-done = bf16[640,384]{1,0:T(8,128)(2,1)} async-done(((bf16[2560,384]{1,0:T(8,128)(2,1)}), bf16[640,384]{1,0:T(8,128)(2,1)}) %reduce-scatter.2.cloned.1.call-update) | async-done | bytes 491536 | tf_op jit(solution)/shard_map/reduce_scatter | solution.py:175
  312.4 3.6 all-to-all-start.1
  316.8 2.4 collective-permute-start.2
  319.2 19.0 %collective-permute-done.2 = f32[32,768]{1,0:T(8,128)S(1)} collective-permute-done((f32[32,768]{1,0:T(8,128)S(1)}, f32[32,768]{1,0:T(8,128)S(1)}, u32[]{:S(2)}, u32[]{:S(2)}) %collective-permute-start.2) | collective-permute-done | bytes 98336 | tf_op jit(solution)/shard_map/ppermute | solution.py:23
  338.7 1.5 collective-permute-start.3
  340.2 3.2 collective-permute-done.3
  343.5 2.5 collective-permute-start.4
  345.9 4.4 %collective-permute-done.4 = f32[32,768]{1,0:T(8,128)S(1)} collective-permute-done((f32[32,768]{1,0:T(8,128)S(1)}, f32[32,768]{1,0:T(8,128)S(1)}, u32[]{:S(2)}, u32[]{:S(2)}) %collective-permute-start.4) | collective-permute-done | bytes 98336 | tf_op jit(solution)/shard_map/ppermute | solution.py:23
  350.3 2.5 collective-permute-start.5
  352.8 7.1 %collective-permute-done.5 = f32[32,768]{1,0:T(8,128)S(1)} collective-permute-done((f32[32,768]{1,0:T(8,128)S(1)}, f32[32,768]{1,0:T(8,128)S(1)}, u32[]{:S(2)}, u32[]{:S(2)}) %collective-permute-start.5) | collective-permute-done | bytes 98336 | tf_op jit(solution)/shard_map/ppermute | solution.py:23
  361.3 3.2 collective-permute-start.7
  364.5 3.3 collective-permute-done.7
  368.3 4.2 %collective-permute-done.8 = f32[32,768]{1,0:T(8,128)S(1)} collective-permute-done((f32[32,768]{1,0:T(8,128)S(1)}, f32[32,768]{1,0:T(8,128)S(1)}, u32[]{:S(2)}, u32[]{:S(2)}) %collective-permute-start.8) | collective-permute-done | bytes 98336 | tf_op jit(solution)/shard_map/ppermute | solution.py:23
  372.5 2.2 collective-permute-start.9
  374.7 4.0 %collective-permute-done.9 = f32[32,768]{1,0:T(8,128)S(1)} collective-permute-done((f32[32,768]{1,0:T(8,128)S(1)}, f32[32,768]{1,0:T(8,128)S(1)}, u32[]{:S(2)}, u32[]{:S(2)}) %collective-permute-start.9) | collective-permute-done | bytes 98336 | tf_op jit(solution)/shard_map/ppermute | solution.py:23
  (220 shorter events, 70.5 us)
Async XLA Ops:
  7.2 4.1 %copy-start.8 = (bf16[160,768]{1,0:T(8,128)(2,1)S(1)}, bf16[160,768]{1,0:T(8,128)(2,1)}, u32[]{:S(2)}) copy-start(bf16[160,768]{1,0:T(8,128)(2,1)} %param.16) | copy-start | bytes 737284
  7.2 4.4 %copy-start.9 = (bf16[160,768]{1,0:T(8,128)(2,1)S(1)}, bf16[160,768]{1,0:T(8,128)(2,1)}, u32[]{:S(2)}) copy-start(bf16[160,768]{1,0:T(8,128)(2,1)} %param.17) | copy-start | bytes 737284
  7.2 81.9 %all-gather.2.cloned.1.call-start = ((), (), s32[]{:S(2)}) async-start(), calls=%async_computation.3 | async-start | bytes 2457600 | tf_op jit(solution)/shard_map/all_gather | solution.py:49
  37.4 127.7 %copy-start.3 = (bf16[1,4,160,1,192]{4,2,0,1,3:T(8,128)(2,1)}, bf16[1,4,160,1,192]{4,2,0,1,3:T(8,128)(2,1)S(1)}, u32[]{:S(2)}) copy-start(bf16[1,4,160,1,192]{4,2,0,1,3:T(8,128)(2,1)S(1)} %get-tuple-element.447) | copy-start | bytes 737284
  38.5 271.2 %reduce-scatter.2.cloned.1.call-start = ((), (), s32[]{:S(2)}) async-start(), calls=%async_computation.4 | async-start | bytes 2457600 | tf_op jit(solution)/shard_map/reduce_scatter | solution.py:175
  40.6 1.2 copy-start.10
  162.7 1.0 copy-start.7
  163.7 8.2 %copy-start.11 = (f32[1,192]{1,0:T(1,128)S(1)}, f32[1,192]{1,0:T(1,128)}, u32[]{:S(2)}) copy-start(f32[1,192]{1,0:T(1,128)} %get-tuple-element.451) | copy-start | bytes 2308
  163.7 8.2 %copy-start.12 = (f32[1,192]{1,0:T(1,128)S(1)}, f32[1,192]{1,0:T(1,128)}, u32[]{:S(2)}) copy-start(f32[1,192]{1,0:T(1,128)} %get-tuple-element.452) | copy-start | bytes 2308
  163.7 8.3 %copy-start.13 = (f32[1,192]{1,0:T(1,128)S(1)}, f32[1,192]{1,0:T(1,128)}, u32[]{:S(2)}) copy-start(f32[1,192]{1,0:T(1,128)} %get-tuple-element.453) | copy-start | bytes 2308
  163.7 8.3 %copy-start.14 = (f32[1,192]{1,0:T(1,128)S(1)}, f32[1,192]{1,0:T(1,128)}, u32[]{:S(2)}) copy-start(f32[1,192]{1,0:T(1,128)} %get-tuple-element.454) | copy-start | bytes 2308
  163.7 8.3 %copy-start.15 = (f32[1,192]{1,0:T(1,128)S(1)}, f32[1,192]{1,0:T(1,128)}, u32[]{:S(2)}) copy-start(f32[1,192]{1,0:T(1,128)} %get-tuple-element.455) | copy-start | bytes 2308
  163.7 8.3 %copy-start.16 = (f32[1,192]{1,0:T(1,128)S(1)}, f32[1,192]{1,0:T(1,128)}, u32[]{:S(2)}) copy-start(f32[1,192]{1,0:T(1,128)} %get-tuple-element.456) | copy-start | bytes 2308
  163.7 8.3 %copy-start.17 = (f32[1,192]{1,0:T(1,128)S(1)}, f32[1,192]{1,0:T(1,128)}, u32[]{:S(2)}) copy-start(f32[1,192]{1,0:T(1,128)} %get-tuple-element.457) | copy-start | bytes 2308
  163.7 8.3 %copy-start.18 = (f32[1,192]{1,0:T(1,128)S(1)}, f32[1,192]{1,0:T(1,128)}, u32[]{:S(2)}) copy-start(f32[1,192]{1,0:T(1,128)} %get-tuple-element.458) | copy-start | bytes 2308
  163.7 8.3 %copy-start.19 = (f32[1,192]{1,0:T(1,128)S(1)}, f32[1,192]{1,0:T(1,128)}, u32[]{:S(2)}) copy-start(f32[1,192]{1,0:T(1,128)} %get-tuple-element.459) | copy-start | bytes 2308
  163.7 8.3 %copy-start.20 = (f32[1,192]{1,0:T(1,128)S(1)}, f32[1,192]{1,0:T(1,128)}, u32[]{:S(2)}) copy-start(f32[1,192]{1,0:T(1,128)} %get-tuple-element.460) | copy-start | bytes 2308
  163.7 8.3 %copy-start.21 = (f32[1,192]{1,0:T(1,128)S(1)}, f32[1,192]{1,0:T(1,128)}, u32[]{:S(2)}) copy-start(f32[1,192]{1,0:T(1,128)} %get-tuple-element.461) | copy-start | bytes 2308
  163.8 8.3 %copy-start.22 = (f32[1,192]{1,0:T(1,128)S(1)}, f32[1,192]{1,0:T(1,128)}, u32[]{:S(2)}) copy-start(f32[1,192]{1,0:T(1,128)} %get-tuple-element.462) | copy-start | bytes 2308
  163.8 8.3 %copy-start.23 = (f32[1,192]{1,0:T(1,128)S(1)}, f32[1,192]{1,0:T(1,128)}, u32[]{:S(2)}) copy-start(f32[1,192]{1,0:T(1,128)} %get-tuple-element.463) | copy-start | bytes 2308
  163.8 8.3 %copy-start.24 = (f32[1,192]{1,0:T(1,128)S(1)}, f32[1,192]{1,0:T(1,128)}, u32[]{:S(2)}) copy-start(f32[1,192]{1,0:T(1,128)} %get-tuple-element.464) | copy-start | bytes 2308
  163.8 8.3 %copy-start.25 = (f32[1,192]{1,0:T(1,128)S(1)}, f32[1,192]{1,0:T(1,128)}, u32[]{:S(2)}) copy-start(f32[1,192]{1,0:T(1,128)} %get-tuple-element.465) | copy-start | bytes 2308
  163.8 8.3 %copy-start.26 = (f32[1,192]{1,0:T(1,128)S(1)}, f32[1,192]{1,0:T(1,128)}, u32[]{:S(2)}) copy-start(f32[1,192]{1,0:T(1,128)} %get-tuple-element.466) | copy-start | bytes 2308
  163.8 8.3 %copy-start.27 = (f32[1,192]{1,0:T(1,128)S(1)}, f32[1,192]{1,0:T(1,128)}, u32[]{:S(2)}) copy-start(f32[1,192]{1,0:T(1,128)} %get-tuple-element.467) | copy-start | bytes 2308
  163.8 8.3 %copy-start.28 = (f32[1,192]{1,0:T(1,128)S(1)}, f32[1,192]{1,0:T(1,128)}, u32[]{:S(2)}) copy-start(f32[1,192]{1,0:T(1,128)} %get-tuple-element.468) | copy-start | bytes 2308
  165.1 6.4 %copy-start.1 = (f32[640,192]{1,0:T(8,128)}, f32[640,192]{1,0:T(8,128)S(1)}, u32[]{:S(2)}) copy-start(f32[640,192]{1,0:T(8,128)S(1)} %copy.87) | copy-start | bytes 1474564
  165.3 6.5 %collective-permute-start = (bf16[31,192]{1,0:T(8,128)(2,1)S(1)}, bf16[31,192]{1,0:T(8,128)(2,1)S(1)}, u32[]{:S(2)}, u32[]{:S(2)}) collective-permute-start(bf16[31,192]{1,0:T(8,128)(2,1)S(1)} %slice.531), channel_id=1, source_target_pairs={{0,4},{4,8},{8,12},{1,5},{5,9},{9,13},{2,6},{6,10},{10,14},{3,7},{... | collective-permute-start | bytes 35720 | tf_op jit(solution)/shard_map/ppermute | solution.py:15
  179.2 10.2 %copy-start.2 = (bf16[640,192]{1,0:T(8,128)(2,1)}, bf16[640,192]{1,0:T(8,128)(2,1)S(1)}, u32[]{:S(2)}) copy-start(bf16[640,192]{1,0:T(8,128)(2,1)S(1)} %get-tuple-element.432) | copy-start | bytes 737284
  179.2 6.9 %collective-permute-start.1 = (bf16[31,192]{1,0:T(8,128)(2,1)S(1)}, bf16[31,192]{1,0:T(8,128)(2,1)S(1)}, u32[]{:S(2)}, u32[]{:S(2)}) collective-permute-start(bf16[31,192]{1,0:T(8,128)(2,1)S(1)} %slice.596), channel_id=1, source_target_pairs={{4,0},{8,4},{12,8},{5,1},{9,5},{13,9},{6,2},{10,6},{14,10},{7,3},{... | collective-permute-start | bytes 35720 | tf_op jit(solution)/shard_map/ppermute | solution.py:15
  186.2 4.0 %copy-start.6 = (f32[640,3,64]{0,2,1:T(8,128)S(1)}, f32[640,3,64]{0,2,1:T(8,128)}, u32[]{:S(2)}) copy-start(f32[640,3,64]{0,2,1:T(8,128)} %get-tuple-element.146) | copy-start | bytes 1474564
  189.3 1.9 copy-start.4
  261.2 2.9 copy-start
  264.2 46.8 %copy-start.5 = (bf16[640,192]{1,0:T(8,128)(2,1)S(1)}, bf16[640,192]{1,0:T(8,128)(2,1)}, u32[]{:S(2)}) copy-start(bf16[640,192]{1,0:T(8,128)(2,1)} %copy-done.4) | copy-start | bytes 737284
  312.3 3.7 copy-start.29
  312.3 3.7 copy-start.30
  312.3 3.8 copy-start.31
  312.3 3.8 copy-start.32
  312.3 3.8 copy-start.33
  312.3 3.8 copy-start.34
  312.3 3.8 copy-start.35
  312.3 3.8 copy-start.36
  312.3 3.8 copy-start.37
  312.3 3.8 copy-start.38
  312.4 3.8 copy-start.39
  312.4 3.8 copy-start.40
  312.4 3.8 copy-start.41
  312.4 3.8 copy-start.42
  312.4 3.8 copy-start.43
  312.4 3.8 copy-start.44
  312.4 3.8 copy-start.45
  312.4 3.8 copy-start.46
  312.4 66.9 %all-to-all-start.1 = ((bf16[5,4,160,1,192]{4,2,3,0,1:T(8,128)(2,1)}), bf16[5,4,160,1,192]{4,2,3,0,1:T(8,128)(2,1)S(1)}, u32[]{:S(2)}, u32[]{:S(2)}) async-start(bf16[5,4,160,1,192]{4,2,3,0,1:T(8,128)(2,1)} %copy.93), calls=%async_computation.2 | async-start | bytes 3276800 | tf_op jit(solution)/shard_map/all_to_all | solution.py:190
  316.8 21.4 %collective-permute-start.2 = (f32[32,768]{1,0:T(8,128)S(1)}, f32[32,768]{1,0:T(8,128)S(1)}, u32[]{:S(2)}, u32[]{:S(2)}) collective-permute-start(f32[32,768]{1,0:T(8,128)S(1)} %dynamic_update_slice.9), channel_id=1, source_target_pairs={{0,1},{1,0},{2,3},{3,2},{4,5},{5,4},{6,7},{7,6},{8,9},{9,8},{10,11... | collective-permute-start | bytes 294920 | tf_op jit(solution)/shard_map/ppermute | solution.py:23
  338.7 4.7 %collective-permute-start.3 = (f32[32,768]{1,0:T(8,128)S(1)}, f32[32,768]{1,0:T(8,128)S(1)}, u32[]{:S(2)}, u32[]{:S(2)}) collective-permute-start(f32[32,768]{1,0:T(8,128)S(1)} %add.364), channel_id=1, source_target_pairs={{0,2},{1,3},{2,0},{3,1},{4,6},{5,7},{6,4},{7,5},{8,10},{9,11},{10,... | collective-permute-start | bytes 294920 | tf_op jit(solution)/shard_map/ppermute | solution.py:23
  343.5 6.8 %collective-permute-start.4 = (f32[32,768]{1,0:T(8,128)S(1)}, f32[32,768]{1,0:T(8,128)S(1)}, u32[]{:S(2)}, u32[]{:S(2)}) collective-permute-start(f32[32,768]{1,0:T(8,128)S(1)} %add.365), channel_id=1, source_target_pairs={{0,4},{4,0},{8,12},{12,8},{1,5},{5,1},{9,13},{13,9},{2,6},{6,2},{1... | collective-permute-start | bytes 294920 | tf_op jit(solution)/shard_map/ppermute | solution.py:23
  350.3 9.6 %collective-permute-start.5 = (f32[32,768]{1,0:T(8,128)S(1)}, f32[32,768]{1,0:T(8,128)S(1)}, u32[]{:S(2)}, u32[]{:S(2)}) collective-permute-start(f32[32,768]{1,0:T(8,128)S(1)} %add.366), channel_id=1, source_target_pairs={{0,8},{4,12},{8,0},{12,4},{1,9},{5,13},{9,1},{13,5},{2,10},{6,14},... | collective-permute-start | bytes 294920 | tf_op jit(solution)/shard_map/ppermute | solution.py:23
  359.9 1.4 collective-permute-start.6
  361.3 6.4 %collective-permute-start.7 = (f32[32,768]{1,0:T(8,128)S(1)}, f32[32,768]{1,0:T(8,128)S(1)}, u32[]{:S(2)}, u32[]{:S(2)}) collective-permute-start(f32[32,768]{1,0:T(8,128)S(1)} %add.368), channel_id=1, source_target_pairs={{0,32},{16,48},{32,0},{48,16},{64,96},{80,112},{96,64},{112,80},{1... | collective-permute-start | bytes 294920 | tf_op jit(solution)/shard_map/ppermute | solution.py:23
  367.8 4.7 %collective-permute-start.8 = (f32[32,768]{1,0:T(8,128)S(1)}, f32[32,768]{1,0:T(8,128)S(1)}, u32[]{:S(2)}, u32[]{:S(2)}) collective-permute-start(f32[32,768]{1,0:T(8,128)S(1)} %add.369), channel_id=1, source_target_pairs={{0,64},{16,80},{32,96},{48,112},{64,0},{80,16},{96,32},{112,48},{1... | collective-permute-start | bytes 294920 | tf_op jit(solution)/shard_map/ppermute | solution.py:23
  372.5 6.2 %collective-permute-start.9 = (f32[32,768]{1,0:T(8,128)S(1)}, f32[32,768]{1,0:T(8,128)S(1)}, u32[]{:S(2)}, u32[]{:S(2)}) collective-permute-start(f32[32,768]{1,0:T(8,128)S(1)} %add.370), channel_id=1, source_target_pairs={{0,128},{16,144},{32,160},{48,176},{64,192},{80,208},{96,224},{112... | collective-permute-start | bytes 294920 | tf_op jit(solution)/shard_map/ppermute | solution.py:23
Sparse Core Ops, SparseCore 0:
  38.6 50.4 all-gather.1
  261.3 48.2 reduce-scatter.1
where the time goes:
time: 395 us; the launch traced here: 393 us
  waiting for transfers between devices  145 us (37%)
  matrix products  71.1 us (18%)
  local copies, waits for them, and re-layouts  59.1 us (15%)
  other arithmetic  52.1 us (13%)
  starting transfers between devices  25 us (6%)
  blocking collectives  24.6 us (6%)
  between operations  15.7 us (4%)
    all_gather x1, waiting for transfers between devices, per_device(): lax.all_gather(jnp.concatenate([mixed[1], mixed[2]], axis=1), 'sa', axis=...  47.3 us
    ppermute x8, waiting for transfers between devices, butterfly_sum(): x = x + lax.ppermute(x, axis, [(i, i ^ step) for i in range(count)])  46.5 us
    reduce_scatter x1, waiting for transfers between devices, per_device(): lax.psum_scatter(grad_terms.reshape(span, 2 * group).astype(jnp.bfloat16)...  44.9 us
    all_to_all x1, blocking collectives, per_device(): lax.all_to_all(stacked.reshape(5, rows, sub_count, group), 'sb', 2, 1, ti...  24.6 us
    dot_general x8, matrix products, block_scores(): jnp.einsum('thd,khd->htk', query_heads, key_part, preferred_element_type=...  23.7 us
    lt x12, other arithmetic, block_scores(): block_start + jnp.arange(key_part.shape[0], dtype=jnp.int32) < length  15.6 us
    dynamic_slice x12, local copies, waits for them, and re-layouts, per_device(): lax.scan(running_total, start_state, (key_blocks, block_starts))  15.6 us
    dynamic_update_slice x8, local copies, waits for them, and re-layouts, per_device(): lax.scan(gradient_block, jnp.zeros((row_count, head_count, HEAD_DIM), jnp...  15.5 us
  transfers between devices with their start and end apart: 13, of which 12 were waited for; matrix products, arithmetic and copies ran while one was open for 2% of the time, Pallas kernels for 0%

commit v1 on v0

--- a/solution.py
+++ b/solution.py
@@ -46,7 +46,15 @@
     queries_b = mixed[0]
     frames_b = mixed[3]
     upstream_b = mixed[4]
-    kv_all = lax.all_gather(jnp.concatenate([mixed[1], mixed[2]], axis=1), "sa", axis=0, tiled=True)
+    kv_all = jnp.concatenate(
+        lax.all_to_all(
+            jnp.stack([jnp.concatenate([mixed[1], mixed[2]], axis=1)] * lax.axis_size("sa")),
+            "sa",
+            0,
+            0,
+        ),
+        axis=0,
+    )
     key_all = kv_all[:, :group]
     value_all = kv_all[:, group:]
     key_block = row_count

time: 395 us -> 394 us (level)
  starting transfers between devices: 25 us -> 41.2 us
  waiting for transfers between devices: 145 us -> 130 us
    all_gather x1 -> x0, waiting for transfers between devices: 47.3 us -> none  [per_device(): lax.all_gather(jnp.concatenate([mixed[1], mixed[2]], axis=1), 'sa', axis=...]
    all_to_all x0 -> x1, waiting for transfers between devices: none -> 32.5 us  [per_device(): lax.all_to_all(jnp.stack([jnp.concatenate([mixed[1], mixed[2]], axis=1)]...]
    ppermute x2, starting transfers between devices: 6.53 us -> 15.4 us  [shifted(): return lax.ppermute(x, axis, pairs)]
    all_to_all x0 -> x1, starting transfers between devices: none -> 7.56 us  [per_device(): lax.all_to_all(jnp.stack([jnp.concatenate([mixed[1], mixed[2]], axis=1)]...]
where the time goes in v1:
time: 394 us; the launch traced here: 392 us
  waiting for transfers between devices  130 us (33%)
  matrix products  68 us (17%)
  local copies, waits for them, and re-layouts  62.6 us (16%)
  other arithmetic  50 us (13%)
  starting transfers between devices  41.2 us (10%)
  blocking collectives  24.6 us (6%)
  between operations  15.7 us (4%)
    ppermute x8, waiting for transfers between devices, butterfly_sum(): x = x + lax.ppermute(x, axis, [(i, i ^ step) for i in range(count)])  46.8 us
    reduce_scatter x1, waiting for transfers between devices, per_device(): lax.psum_scatter(grad_terms.reshape(span, 2 * group).astype(jnp.bfloat16)...  44.8 us
    all_to_all x1, waiting for transfers between devices, per_device(): lax.all_to_all(jnp.stack([jnp.concatenate([mixed[1], mixed[2]], axis=1)]...  32.5 us
    all_to_all x1, blocking collectives, per_device(): lax.all_to_all(stacked.reshape(5, rows, sub_count, group), 'sb', 2, 1, ti...  24.6 us
    dot_general x8, matrix products, block_scores(): jnp.einsum('thd,khd->htk', query_heads, key_part, preferred_element_type=...  23.7 us
    lt x12, other arithmetic, block_scores(): block_start + jnp.arange(key_part.shape[0], dtype=jnp.int32) < length  15.9 us
    dynamic_slice x12, local copies, waits for them, and re-layouts, per_device(): lax.scan(running_total, start_state, (key_blocks, block_starts))  15.8 us
    dynamic_update_slice x8, local copies, waits for them, and re-layouts, per_device(): lax.scan(gradient_block, jnp.zeros((row_count, head_count, HEAD_DIM), jnp...  15.5 us
  transfers between devices with their start and end apart: 13, of which 12 were waited for; matrix products, arithmetic and copies ran while one was open for 2% of the time, Pallas kernels for 0%

profile of v1, /device:TPU:2, one launch (start us, length us, event | category | flops | bytes accessed | tf_op | source)
XLA Modules:
  0.0 392.2 jit_solution(11468851117789124872)
XLA Ops:
  12.6 24.6 %all_to_all.35 = bf16[5,160,4,192]{3,1,0,2:T(8,128)(2,1)S(1)} all-to-all(bf16[5,160,4,192]{3,1,0,2:T(8,128)(2,1)S(1)} %copy.78), channel_id=1, replica_groups=mesh['dp'=16,'sa'=4,'sb'=4] {'sb'}, dimensions={2} | all-to-all | bytes 2457600 | tf_op jit(solution)/shard_map/all_to_all | solution.py:43
  40.1 7.6 %all-to-all-start.1 = ((bf16[4,640,384]{1,2,0:T(8,128)(2,1)}), bf16[4,640,384]{1,2,0:T(8,128)(2,1)}, u32[]{:S(2)}, u32[]{:S(2)}) async-start(bf16[4,640,384]{1,2,0:T(8,128)(2,1)} %stack.146), calls=%async_computation.1 | async-start | bytes 3932160 | tf_op jit(solution)/shard_map/all_to_all | solution.py:50
  50.9 32.5 %all-to-all-done.1 = bf16[4,640,384]{1,2,0:T(8,128)(2,1)} async-done(((bf16[4,640,384]{1,2,0:T(8,128)(2,1)}), bf16[4,640,384]{1,2,0:T(8,128)(2,1)}, u32[]{:S(2)}, u32[]{:S(2)}) %all-to-all-start.1) | async-done | bytes 1966112 | tf_op jit(solution)/shard_map/all_to_all | solution.py:50
  83.3 2.8 copy.80
  86.2 1.6 fusion.111
  87.8 1.6 copy.82
  90.7 41.1 %while.37 = (s32[]{:T(128)}, f32[3,640]{1,0:T(4,128)S(1)}, f32[3,640]{1,0:T(4,128)S(1)}, s32[4]{0:T(128)}, s32[]{:T(128)}, /*index=5*/bf16[4,640,3,64]{1,3,2,0:T...) while((s32[]{:T(128)}, f32[3,640]{1,0:T(4,128)S(1)}, f32[3,640]{1,0:T(4,128)S(1)}, ...), condition=%wide.region_3.4_spmd.clone, body=%wide.region_0.3_spmd.clone.sunk | while | flops 165898880 | bytes 10424316 | solution.py:89
  93.4 4.1 %bitcast_reduce_fusion.2 = (f32[3,640]{1,0:T(4,128)S(1)}, f32[3,640,640]{2,1,0:T(8,128)}) fusion(pred[640]{0:T(1024)(128)(4,1)S(1)} %add_compare_fusion.7, bf16[640,3,64]{0,2,1:T(8,128)(2,1)S(1)} %get-tuple-element.670, bf16[4,640,3,64]{1,3,2,0:T(8,128)(2,1)} %get-tuple-element.669, s32[]{:T(128)} %get-tuple-element.655), kind=kOutput, calls=%fused_computation.1.clone.1 | convolution fusion | flops 160970880 | bytes 5415552 | tf_op jit(solution)/shard_map/while/body/eval_jaxpr/thd,khd->htk/dot_general | solution.py:69
  97.5 3.4 fusion.146
  103.6 4.1 %bitcast_reduce_fusion.2 = (f32[3,640]{1,0:T(4,128)S(1)}, f32[3,640,640]{2,1,0:T(8,128)}) fusion(pred[640]{0:T(1024)(128)(4,1)S(1)} %add_compare_fusion.7, bf16[640,3,64]{0,2,1:T(8,128)(2,1)S(1)} %get-tuple-element.670, bf16[4,640,3,64]{1,3,2,0:T(8,128)(2,1)} %get-tuple-element.669, s32[]{:T(128)} %get-tuple-element.655), kind=kOutput, calls=%fused_computation.1.clone.1 | convolution fusion | flops 160970880 | bytes 5415552 | tf_op jit(solution)/shard_map/while/body/eval_jaxpr/thd,khd->htk/dot_general | solution.py:69
  107.8 3.4 fusion.146
  113.9 4.1 %bitcast_reduce_fusion.2 = (f32[3,640]{1,0:T(4,128)S(1)}, f32[3,640,640]{2,1,0:T(8,128)}) fusion(pred[640]{0:T(1024)(128)(4,1)S(1)} %add_compare_fusion.7, bf16[640,3,64]{0,2,1:T(8,128)(2,1)S(1)} %get-tuple-element.670, bf16[4,640,3,64]{1,3,2,0:T(8,128)(2,1)} %get-tuple-element.669, s32[]{:T(128)} %get-tuple-element.655), kind=kOutput, calls=%fused_computation.1.clone.1 | convolution fusion | flops 160970880 | bytes 5415552 | tf_op jit(solution)/shard_map/while/body/eval_jaxpr/thd,khd->htk/dot_general | solution.py:69
  118.1 3.4 fusion.146
  124.2 4.1 %bitcast_reduce_fusion.2 = (f32[3,640]{1,0:T(4,128)S(1)}, f32[3,640,640]{2,1,0:T(8,128)}) fusion(pred[640]{0:T(1024)(128)(4,1)S(1)} %add_compare_fusion.7, bf16[640,3,64]{0,2,1:T(8,128)(2,1)S(1)} %get-tuple-element.670, bf16[4,640,3,64]{1,3,2,0:T(8,128)(2,1)} %get-tuple-element.669, s32[]{:T(128)} %get-tuple-element.655), kind=kOutput, calls=%fused_computation.1.clone.1 | convolution fusion | flops 160970880 | bytes 5415552 | tf_op jit(solution)/shard_map/while/body/eval_jaxpr/thd,khd->htk/dot_general | solution.py:69
  128.4 3.4 fusion.146
  133.8 22.0 %while.38 = (s32[]{:T(128)}, f32[640,3,64]{0,2,1:T(8,128)S(1)}, bf16[4,640,3,64]{1,3,2,0:T(8,128)(2,1)}, s32[4]{0:T(128)}, s32[]{:T(128)}, /*index=5*/bf16[4,640...) while((s32[]{:T(128)}, f32[640,3,64]{0,2,1:T(8,128)S(1)}, ...), condition=%wide.region_5.6_spmd.clone, body=%wide.region_4.5_spmd.clone.sunk | while | flops 319735040 | bytes 1730435 | solution.py:105
  136.5 2.8 fusion.151
  142.0 2.8 fusion.151
  147.5 2.8 fusion.151
  153.0 2.8 fusion.151
  156.5 14.1 %collective-permute-start = (bf16[31,192]{1,0:T(8,128)(2,1)S(1)}, bf16[31,192]{1,0:T(8,128)(2,1)S(1)}, u32[]{:S(2)}, u32[]{:S(2)}) collective-permute-start(bf16[31,192]{1,0:T(8,128)(2,1)S(1)} %slice.531), channel_id=1, source_target_pairs={{0,4},{4,8},{8,12},{1,5},{5,9},{9,13},{2,6},{6,10},{10,14},{3,7},{... | collective-permute-start | bytes 35720 | tf_op jit(solution)/shard_map/ppermute | solution.py:15
  172.2 7.1 %fusion.71 = (f32[192]{0:T(256)S(1)}, f32[192]{0:T(256)S(1)}, f32[192]{0:T(256)S(1)}, f32[192]{0:T(256)S(1)}, f32[192]{0:T(256)}, /*index=5*/f32[192]{0:T(256)},...) fusion(f32[671,192]{1,0:T(8,128)S(1)} %maximum_convert_fusion, ...), kind=kLoop, calls=%fused_computation.113 | loop fusion | flops 13636224 | bytes 16750720 | tf_op jit(solution)/shard_map/reduce_sum | solution.py:133
  180.6 5.5 %collective-permute-done.1 = bf16[31,192]{1,0:T(8,128)(2,1)S(1)} collective-permute-done((bf16[31,192]{1,0:T(8,128)(2,1)S(1)}, bf16[31,192]{1,0:T(8,128)(2,1)S(1)}, u32[]{:S(2)}, u32[]{:S(2)}) %collective-permute-start.1) | collective-permute-done | bytes 11936 | tf_op jit(solution)/shard_map/ppermute | solution.py:15
  186.2 3.1 fusion.75
  191.2 69.7 %while.39 = (s32[]{:T(128)}, f32[640,3,64]{0,2,1:T(8,128)}, bf16[4,640,384]{2,1,0:T(8,128)(2,1)}, bf16[4,640,3,64]{1,3,2,0:T(8,128)(2,1)}, s32[4]{0:T(128)}, /*i...) while((s32[]{:T(128)}, f32[640,3,64]{0,2,1:T(8,128)}, ...), condition=%wide.region_8.9_spmd.clone, body=%wide.region_7.8_spmd.clone.sunk | while | flops 800195840 | bytes 28289564 | solution.py:178
  191.2 1.8 fusion.162
  195.6 2.7 multiply_convert_fusion.3
  199.2 2.3 fusion.164
  202.3 2.0 copy.135
  204.3 1.8 constant_dynamic-update-slice_fusion.12
  206.2 2.3 fusion.163
  208.5 1.8 fusion.162
  212.9 2.7 multiply_convert_fusion.3
  216.5 2.3 fusion.164
  219.6 2.0 copy.135
  221.6 1.9 constant_dynamic-update-slice_fusion.12
  223.5 2.5 fusion.163
  225.9 1.8 fusion.162
  230.4 2.7 multiply_convert_fusion.3
  234.0 2.3 fusion.164
  237.1 2.0 copy.135
  239.1 1.9 constant_dynamic-update-slice_fusion.12
  241.0 2.5 fusion.163
  243.4 1.8 fusion.162
  247.9 2.7 multiply_convert_fusion.3
  251.5 2.3 fusion.164
  254.6 2.0 copy.135
  256.6 1.9 constant_dynamic-update-slice_fusion.12
  258.4 2.5 fusion.163
  261.0 2.9 fusion.70
  264.5 44.8 %reduce-scatter.2.cloned.1.call-done = bf16[640,384]{1,0:T(8,128)(2,1)} async-done(((bf16[2560,384]{1,0:T(8,128)(2,1)}), bf16[640,384]{1,0:T(8,128)(2,1)}) %reduce-scatter.2.cloned.1.call-update) | async-done | bytes 491536 | tf_op jit(solution)/shard_map/reduce_scatter | solution.py:183
  312.1 3.6 all-to-all-start.2
  316.4 2.4 collective-permute-start.2
  318.8 19.1 %collective-permute-done.2 = f32[32,768]{1,0:T(8,128)S(1)} collective-permute-done((f32[32,768]{1,0:T(8,128)S(1)}, f32[32,768]{1,0:T(8,128)S(1)}, u32[]{:S(2)}, u32[]{:S(2)}) %collective-permute-start.2) | collective-permute-done | bytes 98336 | tf_op jit(solution)/shard_map/ppermute | solution.py:23
  339.9 3.2 collective-permute-done.3
  343.1 2.5 collective-permute-start.4
  345.5 4.4 %collective-permute-done.4 = f32[32,768]{1,0:T(8,128)S(1)} collective-permute-done((f32[32,768]{1,0:T(8,128)S(1)}, f32[32,768]{1,0:T(8,128)S(1)}, u32[]{:S(2)}, u32[]{:S(2)}) %collective-permute-start.4) | collective-permute-done | bytes 98336 | tf_op jit(solution)/shard_map/ppermute | solution.py:23
  349.9 2.5 collective-permute-start.5
  352.5 7.1 %collective-permute-done.5 = f32[32,768]{1,0:T(8,128)S(1)} collective-permute-done((f32[32,768]{1,0:T(8,128)S(1)}, f32[32,768]{1,0:T(8,128)S(1)}, u32[]{:S(2)}, u32[]{:S(2)}) %collective-permute-start.5) | collective-permute-done | bytes 98336 | tf_op jit(solution)/shard_map/ppermute | solution.py:23
  361.0 3.0 collective-permute-start.7
  364.0 3.4 collective-permute-done.7
  367.9 4.2 %collective-permute-done.8 = f32[32,768]{1,0:T(8,128)S(1)} collective-permute-done((f32[32,768]{1,0:T(8,128)S(1)}, f32[32,768]{1,0:T(8,128)S(1)}, u32[]{:S(2)}, u32[]{:S(2)}) %collective-permute-start.8) | collective-permute-done | bytes 98336 | tf_op jit(solution)/shard_map/ppermute | solution.py:23
  372.2 2.1 collective-permute-start.9
  374.3 4.1 %collective-permute-done.9 = f32[32,768]{1,0:T(8,128)S(1)} collective-permute-done((f32[32,768]{1,0:T(8,128)S(1)}, f32[32,768]{1,0:T(8,128)S(1)}, u32[]{:S(2)}, u32[]{:S(2)}) %collective-permute-start.9) | collective-permute-done | bytes 98336 | tf_op jit(solution)/shard_map/ppermute | solution.py:23
  (214 shorter events, 72.7 us)
Async XLA Ops:
  7.2 4.0 %copy-start.8 = (bf16[160,768]{1,0:T(8,128)(2,1)S(1)}, bf16[160,768]{1,0:T(8,128)(2,1)}, u32[]{:S(2)}) copy-start(bf16[160,768]{1,0:T(8,128)(2,1)} %param.16) | copy-start | bytes 737284
  7.2 4.3 %copy-start.9 = (bf16[160,768]{1,0:T(8,128)(2,1)S(1)}, bf16[160,768]{1,0:T(8,128)(2,1)}, u32[]{:S(2)}) copy-start(bf16[160,768]{1,0:T(8,128)(2,1)} %param.17) | copy-start | bytes 737284
  40.1 43.3 %all-to-all-start.1 = ((bf16[4,640,384]{1,2,0:T(8,128)(2,1)}), bf16[4,640,384]{1,2,0:T(8,128)(2,1)}, u32[]{:S(2)}, u32[]{:S(2)}) async-start(bf16[4,640,384]{1,2,0:T(8,128)(2,1)} %stack.146), calls=%async_computation.1 | async-start | bytes 3932160 | tf_op jit(solution)/shard_map/all_to_all | solution.py:50
  47.6 261.7 %reduce-scatter.2.cloned.1.call-start = ((), (), s32[]{:S(2)}) async-start(), calls=%async_computation.4 | async-start | bytes 2457600 | tf_op jit(solution)/shard_map/reduce_scatter | solution.py:183
  49.7 1.2 copy-start.10
  132.4 1.4 copy-start.7
  133.8 22.5 %copy-start.3 = (bf16[1,4,160,1,192]{4,2,0,1,3:T(8,128)(2,1)S(1)}, bf16[1,4,160,1,192]{4,2,0,1,3:T(8,128)(2,1)}, u32[]{:S(2)}) copy-start(bf16[1,4,160,1,192]{4,2,0,1,3:T(8,128)(2,1)} %get-tuple-element.447) | copy-start | bytes 737284
  155.9 16.2 %copy-start.6 = (bf16[1,4,160,1,192]{4,2,0,1,3:T(8,128)(2,1)S(1)}, bf16[1,4,160,1,192]{4,2,0,1,3:T(8,128)(2,1)}, u32[]{:S(2)}) copy-start(bf16[1,4,160,1,192]{4,2,0,1,3:T(8,128)(2,1)} %get-tuple-element.443) | copy-start | bytes 737284
  155.9 16.2 %copy-start.11 = (f32[1,192]{1,0:T(1,128)S(1)}, f32[1,192]{1,0:T(1,128)}, u32[]{:S(2)}) copy-start(f32[1,192]{1,0:T(1,128)} %get-tuple-element.451) | copy-start | bytes 2308
  155.9 16.2 %copy-start.12 = (f32[1,192]{1,0:T(1,128)S(1)}, f32[1,192]{1,0:T(1,128)}, u32[]{:S(2)}) copy-start(f32[1,192]{1,0:T(1,128)} %get-tuple-element.452) | copy-start | bytes 2308
  155.9 16.2 %copy-start.13 = (f32[1,192]{1,0:T(1,128)S(1)}, f32[1,192]{1,0:T(1,128)}, u32[]{:S(2)}) copy-start(f32[1,192]{1,0:T(1,128)} %get-tuple-element.453) | copy-start | bytes 2308
  155.9 16.1 %copy-start.14 = (f32[1,192]{1,0:T(1,128)S(1)}, f32[1,192]{1,0:T(1,128)}, u32[]{:S(2)}) copy-start(f32[1,192]{1,0:T(1,128)} %get-tuple-element.454) | copy-start | bytes 2308
  155.9 16.1 %copy-start.15 = (f32[1,192]{1,0:T(1,128)S(1)}, f32[1,192]{1,0:T(1,128)}, u32[]{:S(2)}) copy-start(f32[1,192]{1,0:T(1,128)} %get-tuple-element.455) | copy-start | bytes 2308
  155.9 16.1 %copy-start.16 = (f32[1,192]{1,0:T(1,128)S(1)}, f32[1,192]{1,0:T(1,128)}, u32[]{:S(2)}) copy-start(f32[1,192]{1,0:T(1,128)} %get-tuple-element.456) | copy-start | bytes 2308
  155.9 16.1 %copy-start.17 = (f32[1,192]{1,0:T(1,128)S(1)}, f32[1,192]{1,0:T(1,128)}, u32[]{:S(2)}) copy-start(f32[1,192]{1,0:T(1,128)} %get-tuple-element.457) | copy-start | bytes 2308
  155.9 16.1 %copy-start.18 = (f32[1,192]{1,0:T(1,128)S(1)}, f32[1,192]{1,0:T(1,128)}, u32[]{:S(2)}) copy-start(f32[1,192]{1,0:T(1,128)} %get-tuple-element.458) | copy-start | bytes 2308
  156.0 16.1 %copy-start.19 = (f32[1,192]{1,0:T(1,128)S(1)}, f32[1,192]{1,0:T(1,128)}, u32[]{:S(2)}) copy-start(f32[1,192]{1,0:T(1,128)} %get-tuple-element.459) | copy-start | bytes 2308
  156.0 16.1 %copy-start.20 = (f32[1,192]{1,0:T(1,128)S(1)}, f32[1,192]{1,0:T(1,128)}, u32[]{:S(2)}) copy-start(f32[1,192]{1,0:T(1,128)} %get-tuple-element.460) | copy-start | bytes 2308
  156.0 16.1 %copy-start.21 = (f32[1,192]{1,0:T(1,128)S(1)}, f32[1,192]{1,0:T(1,128)}, u32[]{:S(2)}) copy-start(f32[1,192]{1,0:T(1,128)} %get-tuple-element.461) | copy-start | bytes 2308
  156.0 16.1 %copy-start.22 = (f32[1,192]{1,0:T(1,128)S(1)}, f32[1,192]{1,0:T(1,128)}, u32[]{:S(2)}) copy-start(f32[1,192]{1,0:T(1,128)} %get-tuple-element.462) | copy-start | bytes 2308
  156.0 16.1 %copy-start.23 = (f32[1,192]{1,0:T(1,128)S(1)}, f32[1,192]{1,0:T(1,128)}, u32[]{:S(2)}) copy-start(f32[1,192]{1,0:T(1,128)} %get-tuple-element.463) | copy-start | bytes 2308
  156.0 16.1 %copy-start.24 = (f32[1,192]{1,0:T(1,128)S(1)}, f32[1,192]{1,0:T(1,128)}, u32[]{:S(2)}) copy-start(f32[1,192]{1,0:T(1,128)} %get-tuple-element.464) | copy-start | bytes 2308
  156.0 16.1 %copy-start.25 = (f32[1,192]{1,0:T(1,128)S(1)}, f32[1,192]{1,0:T(1,128)}, u32[]{:S(2)}) copy-start(f32[1,192]{1,0:T(1,128)} %get-tuple-element.465) | copy-start | bytes 2308
  156.0 16.1 %copy-start.26 = (f32[1,192]{1,0:T(1,128)S(1)}, f32[1,192]{1,0:T(1,128)}, u32[]{:S(2)}) copy-start(f32[1,192]{1,0:T(1,128)} %get-tuple-element.466) | copy-start | bytes 2308
  156.0 16.1 %copy-start.27 = (f32[1,192]{1,0:T(1,128)S(1)}, f32[1,192]{1,0:T(1,128)}, u32[]{:S(2)}) copy-start(f32[1,192]{1,0:T(1,128)} %get-tuple-element.467) | copy-start | bytes 2308
  156.0 16.1 %copy-start.28 = (f32[1,192]{1,0:T(1,128)S(1)}, f32[1,192]{1,0:T(1,128)}, u32[]{:S(2)}) copy-start(f32[1,192]{1,0:T(1,128)} %get-tuple-element.468) | copy-start | bytes 2308
  156.3 15.3 %copy-start.1 = (f32[640,192]{1,0:T(8,128)}, f32[640,192]{1,0:T(8,128)S(1)}, u32[]{:S(2)}) copy-start(f32[640,192]{1,0:T(8,128)S(1)} %copy.87) | copy-start | bytes 1474564
  156.5 15.4 %collective-permute-start = (bf16[31,192]{1,0:T(8,128)(2,1)S(1)}, bf16[31,192]{1,0:T(8,128)(2,1)S(1)}, u32[]{:S(2)}, u32[]{:S(2)}) collective-permute-start(bf16[31,192]{1,0:T(8,128)(2,1)S(1)} %slice.531), channel_id=1, source_target_pairs={{0,4},{4,8},{8,12},{1,5},{5,9},{9,13},{2,6},{6,10},{10,14},{3,7},{... | collective-permute-start | bytes 35720 | tf_op jit(solution)/shard_map/ppermute | solution.py:15
  179.3 10.0 %copy-start.2 = (bf16[640,192]{1,0:T(8,128)(2,1)}, bf16[640,192]{1,0:T(8,128)(2,1)S(1)}, u32[]{:S(2)}) copy-start(bf16[640,192]{1,0:T(8,128)(2,1)S(1)} %get-tuple-element.432) | copy-start | bytes 737284
  179.3 6.8 %collective-permute-start.1 = (bf16[31,192]{1,0:T(8,128)(2,1)S(1)}, bf16[31,192]{1,0:T(8,128)(2,1)S(1)}, u32[]{:S(2)}, u32[]{:S(2)}) collective-permute-start(bf16[31,192]{1,0:T(8,128)(2,1)S(1)} %slice.596), channel_id=1, source_target_pairs={{4,0},{8,4},{12,8},{5,1},{9,5},{13,9},{6,2},{10,6},{14,10},{7,3},{... | collective-permute-start | bytes 35720 | tf_op jit(solution)/shard_map/ppermute | solution.py:15
  189.3 1.9 copy-start.4
  260.9 2.9 copy-start
  263.9 46.7 %copy-start.5 = (bf16[640,192]{1,0:T(8,128)(2,1)S(1)}, bf16[640,192]{1,0:T(8,128)(2,1)}, u32[]{:S(2)}) copy-start(bf16[640,192]{1,0:T(8,128)(2,1)} %copy-done.4) | copy-start | bytes 737284
  311.9 3.7 copy-start.29
  311.9 3.7 copy-start.30
  312.0 3.7 copy-start.31
  312.0 3.7 copy-start.32
  312.0 3.7 copy-start.33
  312.0 3.7 copy-start.34
  312.0 3.7 copy-start.35
  312.0 3.7 copy-start.36
  312.0 3.7 copy-start.37
  312.0 3.7 copy-start.38
  312.0 3.7 copy-start.39
  312.0 3.7 copy-start.40
  312.0 3.7 copy-start.41
  312.1 3.7 copy-start.42
  312.1 67.0 %all-to-all-start.2 = ((bf16[5,4,160,1,192]{4,2,3,0,1:T(8,128)(2,1)}), bf16[5,4,160,1,192]{4,2,3,0,1:T(8,128)(2,1)S(1)}, u32[]{:S(2)}, u32[]{:S(2)}) async-start(bf16[5,4,160,1,192]{4,2,3,0,1:T(8,128)(2,1)} %copy.93), calls=%async_computation.3 | async-start | bytes 3276800 | tf_op jit(solution)/shard_map/all_to_all | solution.py:198
  316.4 21.5 %collective-permute-start.2 = (f32[32,768]{1,0:T(8,128)S(1)}, f32[32,768]{1,0:T(8,128)S(1)}, u32[]{:S(2)}, u32[]{:S(2)}) collective-permute-start(f32[32,768]{1,0:T(8,128)S(1)} %dynamic_update_slice.9), channel_id=1, source_target_pairs={{0,1},{1,0},{2,3},{3,2},{4,5},{5,4},{6,7},{7,6},{8,9},{9,8},{10,11... | collective-permute-start | bytes 294920 | tf_op jit(solution)/shard_map/ppermute | solution.py:23
  338.4 4.7 %collective-permute-start.3 = (f32[32,768]{1,0:T(8,128)S(1)}, f32[32,768]{1,0:T(8,128)S(1)}, u32[]{:S(2)}, u32[]{:S(2)}) collective-permute-start(f32[32,768]{1,0:T(8,128)S(1)} %add.364), channel_id=1, source_target_pairs={{0,2},{1,3},{2,0},{3,1},{4,6},{5,7},{6,4},{7,5},{8,10},{9,11},{10,... | collective-permute-start | bytes 294920 | tf_op jit(solution)/shard_map/ppermute | solution.py:23
  343.1 6.8 %collective-permute-start.4 = (f32[32,768]{1,0:T(8,128)S(1)}, f32[32,768]{1,0:T(8,128)S(1)}, u32[]{:S(2)}, u32[]{:S(2)}) collective-permute-start(f32[32,768]{1,0:T(8,128)S(1)} %add.365), channel_id=1, source_target_pairs={{0,4},{4,0},{8,12},{12,8},{1,5},{5,1},{9,13},{13,9},{2,6},{6,2},{1... | collective-permute-start | bytes 294920 | tf_op jit(solution)/shard_map/ppermute | solution.py:23
  349.9 9.6 %collective-permute-start.5 = (f32[32,768]{1,0:T(8,128)S(1)}, f32[32,768]{1,0:T(8,128)S(1)}, u32[]{:S(2)}, u32[]{:S(2)}) collective-permute-start(f32[32,768]{1,0:T(8,128)S(1)} %add.366), channel_id=1, source_target_pairs={{0,8},{4,12},{8,0},{12,4},{1,9},{5,13},{9,1},{13,5},{2,10},{6,14},... | collective-permute-start | bytes 294920 | tf_op jit(solution)/shard_map/ppermute | solution.py:23
  359.6 1.4 collective-permute-start.6
  361.0 6.4 %collective-permute-start.7 = (f32[32,768]{1,0:T(8,128)S(1)}, f32[32,768]{1,0:T(8,128)S(1)}, u32[]{:S(2)}, u32[]{:S(2)}) collective-permute-start(f32[32,768]{1,0:T(8,128)S(1)} %add.368), channel_id=1, source_target_pairs={{0,32},{16,48},{32,0},{48,16},{64,96},{80,112},{96,64},{112,80},{1... | collective-permute-start | bytes 294920 | tf_op jit(solution)/shard_map/ppermute | solution.py:23
  367.4 4.7 %collective-permute-start.8 = (f32[32,768]{1,0:T(8,128)S(1)}, f32[32,768]{1,0:T(8,128)S(1)}, u32[]{:S(2)}, u32[]{:S(2)}) collective-permute-start(f32[32,768]{1,0:T(8,128)S(1)} %add.369), channel_id=1, source_target_pairs={{0,64},{16,80},{32,96},{48,112},{64,0},{80,16},{96,32},{112,48},{1... | collective-permute-start | bytes 294920 | tf_op jit(solution)/shard_map/ppermute | solution.py:23
  372.2 6.2 %collective-permute-start.9 = (f32[32,768]{1,0:T(8,128)S(1)}, f32[32,768]{1,0:T(8,128)S(1)}, u32[]{:S(2)}, u32[]{:S(2)}) collective-permute-start(f32[32,768]{1,0:T(8,128)S(1)} %add.370), channel_id=1, source_target_pairs={{0,128},{16,144},{32,160},{48,176},{64,192},{80,208},{96,224},{112... | collective-permute-start | bytes 294920 | tf_op jit(solution)/shard_map/ppermute | solution.py:23
Sparse Core Ops, SparseCore 0:
  261.1 48.1 reduce-scatter.1
